TPU v7x, 32 devices: a whole 2x2x4 slice. The times are simulated.
32 devices in a mesh: seq: 8 (over y, x, core), tp: 4 (over z).
Axes of the slice: x: 2, y: 2, z: 4, core: 2. Of those that a mesh axis runs over, the one named last changes fastest.
Arguments:
- projected: bfloat16 [1536, 3, 8192], P('seq', None, 'tp'), may hold values from -6 to 6
- feat_taps: float32 [7, 3, 8192], P(None, None, 'tp'), may hold values from -2.5 to 2.5
- filters: float32 [512, 128], P('tp'), may hold values from -1.5 to 1.5
- out_weight: bfloat16 [8192, 8192], P('tp'), may hold values from -0.09375 to 0.09375
- cotangent: bfloat16 [1536, 8192], P('seq', 'tp'), may hold values from -6 to 6
Outputs:
- output: bfloat16 [1536, 8192], P('seq', 'tp')
- input_grad: bfloat16 [1536, 3, 8192], P('seq', None, 'tp')
All inputs are finite; a program needn't handle non-finite values.
Results may differ from a plain program's by a relative error of at most 0.0095.
Values may be sent and summed in bfloat16 or wider, within the bound.
No kernel may reach another device: no remote copies, remote signals or barrier semaphores. Data moves between devices by JAX's collectives and lax.ppermute only.
A program may use at most 128 MiB of HBM per device.

v0:
```python
import jax
import jax.numpy as jnp
from jax import lax
from jax.sharding import PartitionSpec as P


def take_rows(source, start, count, time_axis):
    return lax.slice_in_dim(source, start, start + count, axis=time_axis)


def component(source, index):
    return source[index]


def causal_taps(extended, weights, out_rows, time_axis):
    tap_count = weights.shape[0]
    result = weights[0] * take_rows(extended, tap_count - 1, out_rows, time_axis)
    for delay in range(1, tap_count):
        result = result + weights[delay] * take_rows(
            extended, tap_count - 1 - delay, out_rows, time_axis
        )
    return result


def later_taps(extended, weights, out_rows, time_axis):
    result = weights[0] * take_rows(extended, 0, out_rows, time_axis)
    for delay in range(1, weights.shape[0]):
        result = result + weights[delay] * take_rows(extended, delay, out_rows, time_axis)
    return result


def forward_core(extended, feat_weights, kernel_taps, row_count):
    filt_len = kernel_taps.shape[0]
    stack_axis = extended.ndim - 1
    plain_axis = 1
    feats = causal_taps(extended, feat_weights, row_count + filt_len - 1, stack_axis)
    product = component(feats, 1) * component(feats, 2)
    conv = causal_taps(product, kernel_taps, row_count, plain_axis)
    tail_rows = take_rows(feats, filt_len - 1, row_count, stack_axis)
    query = component(tail_rows, 0)
    mixed = (query * conv).astype(jnp.bfloat16)
    return (mixed, query, conv, component(tail_rows, 1), component(tail_rows, 2))


def backward_core(
    signal_ext, query_ext, key_ext, value_ext, feat_weights, kernel_taps, row_count, mixed_rows
):
    feat_len = feat_weights.shape[0]
    plain_axis = 1
    conv_grad = later_taps(signal_ext, kernel_taps, mixed_rows, plain_axis)
    padding = [(0, 0), (0, 0)]
    padding[plain_axis] = (0, row_count + feat_len - 1 - mixed_rows)
    conv_grad = jnp.pad(conv_grad, padding)
    stacked = jnp.stack([query_ext, conv_grad * value_ext, conv_grad * key_ext], axis=0)
    stack_axis = 2
    return later_taps(stacked, feat_weights, row_count, stack_axis).astype(jnp.bfloat16)


def body(projected, feat_taps, filters, out_weight, cotangent):
    channels = projected.shape[2]
    feat_len = feat_taps.shape[0]
    filt_len = filters.shape[1]
    reach = filt_len + feat_len - 2
    group_size = channels // filters.shape[0]
    channel_kernel = jnp.repeat(filters, group_size, axis=0)
    shards = lax.axis_size("seq")
    slim = channels // shards
    position = lax.axis_index("seq")
    moved = jnp.transpose(projected, (1, 2, 0))
    regrouped = lax.all_to_all(moved, "seq", split_axis=1, concat_axis=2, tiled=True)
    seq_rows = regrouped.shape[2]
    local_kernel = lax.dynamic_slice_in_dim(channel_kernel, position * slim, slim, 0)
    kernel_taps = local_kernel.T[:, :, None]
    local_taps = lax.dynamic_slice_in_dim(feat_taps, position * slim, slim, 2)[..., None]
    extended = jnp.pad(regrouped, ((0, 0), (0, 0), (reach, 0)))
    mixed_part, query, conv, key_feat, value_feat = forward_core(
        extended, local_taps, kernel_taps, seq_rows
    )
    mixed = lax.all_to_all(mixed_part, "seq", split_axis=1, concat_axis=0, tiled=True)
    mixed_form = "cd,ct->dt"
    weight_cols = out_weight
    summed = lax.psum_scatter(
        jnp.einsum(mixed_form, weight_cols, mixed, preferred_element_type=jnp.float32).astype(
            jnp.bfloat16
        ),
        "tp",
        scatter_dimension=0,
        tiled=True,
    ).astype(jnp.float32)
    output = summed.T.astype(jnp.bfloat16)
    grad_form = "te,ce->ct"
    weight_cols = out_weight
    grad_mixed = jnp.einsum(
        grad_form,
        lax.all_gather(cotangent, "tp", axis=1, tiled=True),
        weight_cols,
        preferred_element_type=jnp.float32,
    )
    grad_part = lax.all_to_all(grad_mixed, "seq", split_axis=0, concat_axis=1, tiled=True)
    signal_grad = grad_part * query
    query_grad = grad_part * conv
    tail_pad = ((0, 0), (0, feat_len - 1))
    signal_ext = jnp.pad(signal_grad, ((0, 0), (0, filt_len - 1)))
    input_part = backward_core(
        signal_ext,
        jnp.pad(query_grad, tail_pad),
        jnp.pad(key_feat, tail_pad),
        jnp.pad(value_feat, tail_pad),
        local_taps,
        kernel_taps,
        seq_rows,
        seq_rows,
    )
    returned = lax.all_to_all(input_part, "seq", split_axis=2, concat_axis=1, tiled=True)
    input_grad = jnp.transpose(returned, (2, 0, 1))
    return (output, input_grad)


def solution(mesh):
    in_specs = (
        P("seq", None, "tp"),
        P(None, None, "tp"),
        P("tp", None),
        P("tp", None),
        P("seq", "tp"),
    )
    out_specs = (P("seq", "tp"), P("seq", None, "tp"))
    return jax.shard_map(body, mesh=mesh, in_specs=in_specs, out_specs=out_specs, check_vma=False)
```

profile of v0, /device:TPU:0, one launch (start us, length us, event | category | flops | bytes accessed | tf_op | source)
XLA Modules:
  0.0 311.3 jit_solution(12875204798442375766)
XLA Ops:
  7.9 6.9 %copy.14 = bf16[192,3,2048]{0,1,2:T(4,128)(2,1)} copy(bf16[192,3,2048]{2,0,1:T(8,128)(2,1)} %param.5) | data formatting | bytes 4718592 | tf_op args[0]
  14.9 5.2 %all-to-all-start = ((bf16[3,2048,192]{2,0,1:T(4,128)(2,1)}), bf16[3,2048,192]{2,0,1:T(4,128)(2,1)}, u32[]{:S(2)}, u32[]{:S(2)}) async-start(bf16[3,2048,192]{2,0,1:T(4,128)(2,1)} %bitcast.69), calls=%async_computation | async-start | bytes 8388608 | tf_op jit(solution)/shard_map/all_to_all | solution.py:70
  25.3 2.0 slice_reduce_fusion.126
  27.3 2.0 slice_reduce_fusion.125
  29.3 2.0 slice_reduce_fusion.124
  31.3 2.0 slice_reduce_fusion.123
  33.3 36.0 %all-to-all-done = bf16[3,2048,192]{2,0,1:T(4,128)(2,1)} async-done(((bf16[3,2048,192]{2,0,1:T(4,128)(2,1)}), bf16[3,2048,192]{2,0,1:T(4,128)(2,1)}, u32[]{:S(2)}, u32[]{:S(2)}) %all-to-all-start) | async-done | bytes 2359328 | tf_op jit(solution)/shard_map/all_to_all | solution.py:70
  69.3 6.9 %copy.23 = bf16[3,8,256,192]{2,3,1,0:T(8,128)(2,1)} copy(bf16[3,8,256,192]{3,0,2,1:T(4,128)(2,1)} %bitcast.1) | data formatting | bytes 4718592 | tf_op jit(solution)/shard_map/all_to_all | solution.py:70
  76.2 18.0 %fusion.143 = f32[2048,192]{0,1:T(8,128)S(1)} fusion(bf16[2048,8192]{1,0:T(8,128)(2,1)} %param.8, bf16[192,8192]{1,0:T(8,128)(2,1)} %all-gather.2.cloned.1.call-done), kind=kOutput, calls=%fused_computation.438 | convolution fusion | flops 6442450944 | bytes 38273024 | tf_op jit(solution)/shard_map/te,ce->ct/dot_general | solution.py:93
  95.5 3.6 %all-to-all-start.2 = ((f32[8,256,192]{1,2,0:T(8,128)}), f32[8,256,192]{1,2,0:T(8,128)S(1)}, u32[]{:S(2)}, u32[]{:S(2)}) async-start(f32[8,256,192]{1,2,0:T(8,128)} %bitcast.67), calls=%async_computation.3 | async-start | bytes 3145728 | tf_op jit(solution)/shard_map/all_to_all | solution.py:99
  99.1 10.0 %multiply_add_fusion = f32[3,256,1663]{1,2,0:T(8,128)S(1)} fusion(f32[3,256]{1,0:T(4,128)S(1)} %get-tuple-element.145, f32[3,256]{1,0:T(4,128)S(1)} %get-tuple-element.146, f32[3,256]{1,0:T(4,128)S(1)} %get-tuple-element.147, f32[3,256]{1,0:T(4,128)S(1)} %get-tuple-element.148, f32[3,256]{1,0:T(4,128)S(1)} %get-tuple-element.149, ...), kind=kLoop, calls=%fused_computation.2 | loop fusion | flops 25543680 | bytes 7489536 | tf_op jit(solution)/shard_map/add | solution.py:19
  109.1 2.2 copy-done.2
  111.6 8.4 %all-to-all-done.2 = f32[8,256,192]{1,2,0:T(8,128)S(1)} async-done(((f32[8,256,192]{1,2,0:T(8,128)}), f32[8,256,192]{1,2,0:T(8,128)S(1)}, u32[]{:S(2)}, u32[]{:S(2)}) %all-to-all-start.2) | async-done | bytes 1572896 | tf_op jit(solution)/shard_map/all_to_all | solution.py:99
  120.0 41.9 %bitcast_multiply_fusion.1 = (f32[256,1536]{0,1:T(8,128)}, f32[256,1536]{0,1:T(8,128)}) fusion(f32[8,256,192]{1,2,0:T(8,128)S(1)} %all-to-all-done.2, f32[256,1663]{0,1:T(8,128)S(1)} %fusion.8, f32[256]{0:T(256)S(1)} %get-tuple-element.3, f32[256]{0:T(256)S(1)} %get-tuple-element.4, f32[256]{0:T(256)S(1)} %get-tuple-element.5, f32[256]{0:T(256)S(1)} %get-tuple-element.6, ...), kind=kLoop, calls=%fused_computation.283 | loop fusion | flops 100663296 | bytes 206176256 | tf_op jit(solution)/shard_map/mul | solution.py:101
  161.9 3.2 %bitcast_multiply_fusion = (f32[256,1536]{0,1:T(8,128)S(1)}, bf16[256,1536]{0,1:T(8,128)(2,1)}) fusion(f32[8,256,192]{1,2,0:T(8,128)S(1)} %all-to-all-done.2, f32[3,256,1663]{1,2,0:T(8,128)} %copy-done.2, f32[256,1536]{0,1:T(8,128)} %get-tuple-element.131), kind=kLoop, calls=%fused_computation.282 | loop fusion | flops 1179648 | bytes 7077888 | tf_op jit(solution)/shard_map/mul | solution.py:100
  165.2 3.8 %all-to-all-start.1 = ((bf16[256,8,192]{0,2,1:T(8,128)(2,1)}), bf16[256,8,192]{0,2,1:T(8,128)(2,1)S(1)}, u32[]{:S(2)}, u32[]{:S(2)}) async-start(bf16[256,8,192]{0,2,1:T(8,128)(2,1)} %bitcast.72), calls=%async_computation.1 | async-start | bytes 1572864 | tf_op jit(solution)/shard_map/all_to_all | solution.py:79
  169.0 3.7 %slice_bitcast_fusion.1 = (f32[256,1536]{0,1:T(8,128)}, f32[256,1536]{0,1:T(8,128)}) fusion(f32[3,256,1663]{1,2,0:T(8,128)} %copy-done.2), kind=kLoop, calls=%fused_computation.25 | loop fusion | bytes 6291456 | tf_op jit(solution)/shard_map/squeeze | solution.py:12
  172.7 8.7 %all-to-all-done.1 = bf16[256,8,192]{0,2,1:T(8,128)(2,1)S(1)} async-done(((bf16[256,8,192]{0,2,1:T(8,128)(2,1)}), bf16[256,8,192]{0,2,1:T(8,128)(2,1)S(1)}, u32[]{:S(2)}, u32[]{:S(2)}) %all-to-all-start.1) | async-done | bytes 786464 | tf_op jit(solution)/shard_map/all_to_all | solution.py:79
  181.5 15.7 %fusion = bf16[8192,192]{0,1:T(8,128)(2,1)} fusion(bf16[2048,192]{0,1:T(8,128)(2,1)S(1)} %bitcast.77, bf16[2048,8192]{1,0:T(8,128)(2,1)} %param.8), kind=kOutput, calls=%fused_computation.1 | convolution fusion | flops 6444023808 | bytes 37486592 | tf_op jit(solution)/shard_map/cd,ct->dt/dot_general | solution.py:83
  198.2 43.8 %multiply_add_fusion.1 = f32[256,1536]{0,1:T(8,128)} fusion(f32[256,1536]{0,1:T(8,128)S(1)} %get-tuple-element.134, f32[256]{0:T(256)S(1)} %get-tuple-element.3, f32[256]{0:T(256)S(1)} %get-tuple-element.4, f32[256]{0:T(256)S(1)} %get-tuple-element.5, f32[256]{0:T(256)S(1)} %get-tuple-element.6, f32[256]{0:T(256)S(1)} %get-tuple-element.7, ...), kind=kLoop, calls=%fused_computation.284 | loop fusion | flops 100270080 | bytes 3276800 | tf_op jit(solution)/shard_map/add | solution.py:28
  246.0 4.0 %fusion.2 = bf16[3,256,1536]{1,2,0:T(8,128)(2,1)S(1)} fusion(f32[3,256,1542]{1,2,0:T(8,128)S(1)} %pad_maximum_fusion, f32[3,256]{1,0:T(4,128)S(1)} %get-tuple-element.145, f32[3,256]{1,0:T(4,128)S(1)} %get-tuple-element.146, f32[3,256]{1,0:T(4,128)S(1)} %get-tuple-element.147, f32[3,256]{1,0:T(4,128)S(1)} %get-tuple-element.148, ...), kind=kLoop, calls=%fused_computation.6 | loop fusion | flops 16515072 | bytes 35410944 | tf_op jit(solution)/shard_map/convert_element_type | solution.py:56
  250.0 12.0 %copy.19 = bf16[3,256,1536]{1,0,2:T(4,128)(2,1)S(1)} copy(bf16[3,256,1536]{1,2,0:T(8,128)(2,1)S(1)} %fusion.2) | data formatting | bytes 4718592 | tf_op jit(solution)/shard_map/convert_element_type | solution.py:56
  262.1 40.3 %all_to_all.74 = bf16[3,256,1536]{1,0,2:T(4,128)(2,1)S(1)} all-to-all(bf16[3,256,1536]{1,0,2:T(4,128)(2,1)S(1)} %copy.19), channel_id=1, replica_groups=mesh['seq'=8,'tp'=4] {'seq'}, dimensions={2} | all-to-all | bytes 4718592 | tf_op jit(solution)/shard_map/all_to_all | solution.py:114
  302.7 1.7 copy.33
  (98 shorter events, 12.5 us)
Async XLA Ops:
  7.2 14.1 %copy-start = (f32[128,128]{1,0:T(8,128)S(1)}, f32[128,128]{1,0:T(8,128)}, u32[]{:S(2)}) copy-start(f32[128,128]{1,0:T(8,128)} %param.7) | copy-start | bytes 196612
  7.2 69.0 %all-gather.2.cloned.1.call-start = ((), (), s32[]{:S(2)}) async-start(), calls=%async_computation.6 | async-start | bytes 3932160 | tf_op jit(solution)/shard_map/all_gather | solution.py:95
  14.9 54.4 %all-to-all-start = ((bf16[3,2048,192]{2,0,1:T(4,128)(2,1)}), bf16[3,2048,192]{2,0,1:T(4,128)(2,1)}, u32[]{:S(2)}, u32[]{:S(2)}) async-start(bf16[3,2048,192]{2,0,1:T(4,128)(2,1)} %bitcast.69), calls=%async_computation | async-start | bytes 8388608 | tf_op jit(solution)/shard_map/all_to_all | solution.py:70
  95.5 24.5 %all-to-all-start.2 = ((f32[8,256,192]{1,2,0:T(8,128)}), f32[8,256,192]{1,2,0:T(8,128)S(1)}, u32[]{:S(2)}, u32[]{:S(2)}) async-start(f32[8,256,192]{1,2,0:T(8,128)} %bitcast.67), calls=%async_computation.3 | async-start | bytes 3145728 | tf_op jit(solution)/shard_map/all_to_all | solution.py:99
  109.1 2.3 copy-start.2
  165.2 16.3 %all-to-all-start.1 = ((bf16[256,8,192]{0,2,1:T(8,128)(2,1)}), bf16[256,8,192]{0,2,1:T(8,128)(2,1)S(1)}, u32[]{:S(2)}, u32[]{:S(2)}) async-start(bf16[256,8,192]{0,2,1:T(8,128)(2,1)} %bitcast.72), calls=%async_computation.1 | async-start | bytes 1572864 | tf_op jit(solution)/shard_map/all_to_all | solution.py:79
  168.9 135.5 %reduce-scatter.2.cloned.1.call-start = ((), (), s32[]{:S(2)}) async-start(), calls=%async_computation.5 | async-start | bytes 3932160 | tf_op jit(solution)/shard_map/reduce_scatter | solution.py:82
  197.3 0.7 copy-start.9
  197.3 0.7 copy-start.10
  197.3 0.7 copy-start.11
  197.3 0.7 copy-start.12
  197.3 0.7 copy-start.13
  197.3 0.7 copy-start.14
  197.3 0.7 copy-start.15
  197.3 0.7 copy-start.16
  197.4 0.7 copy-start.19
  197.5 0.7 copy-start.33
  197.5 0.7 copy-start.34
  197.5 0.7 copy-start.35
  197.6 0.7 copy-start.37
  198.2 43.8 %copy-start.3 = (f32[256,1536]{0,1:T(8,128)S(1)}, f32[256,1536]{0,1:T(8,128)}, u32[]{:S(2)}) copy-start(f32[256,1536]{0,1:T(8,128)} %get-tuple-element.130) | copy-start | bytes 4718596
  242.0 1.4 copy-start.4
  242.0 1.9 copy-start.5
  302.7 1.7 copy-start.1
  (19 other events, 12.6 us)
Sparse Core Ops, SparseCore 0:
  9.6 66.1 all-gather.1
  197.7 60.5 reduce-scatter.1
where the time goes:
time: 312 us; the launch traced here: 311 us
  other arithmetic  105 us (34%)
  waiting for transfers between devices  53.9 us (17%)
  local copies, waits for them, and re-layouts  51 us (16%)
  blocking collectives  40.3 us (13%)
  matrix products  33.7 us (11%)
  between operations  14.6 us (5%)
  starting transfers between devices  12.6 us (4%)
    add x1, other arithmetic, later_taps(): result + weights[delay] * take_rows(extended, delay, out_rows, time_axis)  43.8 us
    mul x1, other arithmetic, body(): query_grad = grad_part * conv  41.9 us
    all_to_all x1, blocking collectives, body(): lax.all_to_all(input_part, 'seq', split_axis=2, concat_axis=1, tiled=True)  40.3 us
    all_to_all x1, waiting for transfers between devices, body(): lax.all_to_all(moved, 'seq', split_axis=1, concat_axis=2, tiled=True)  36 us
    dot_general x1, matrix products, body(): jnp.einsum(grad_form, lax.all_gather(cotangent, 'tp', axis=1, tiled=True)...  18 us
    dot_general x1, matrix products, body(): jnp.einsum(mixed_form, weight_cols, mixed, preferred_element_type=jnp.flo...  15.7 us
    convert_element_type x1, local copies, waits for them, and re-layouts, backward_core(): later_taps(stacked, feat_weights, row_count, stack_axis)  12 us
    unnamed x81, local copies, waits for them, and re-layouts  11.6 us
  transfers between devices with their start and end apart: 5, of which 3 were waited for; matrix products, arithmetic and copies ran while one was open for 34% of the time, Pallas kernels for 0%

commit v1 on v0

--- a/solution.py
+++ b/solution.py
@@ -76,7 +76,10 @@
     mixed_part, query, conv, key_feat, value_feat = forward_core(
         extended, local_taps, kernel_taps, seq_rows
     )
-    mixed = lax.all_to_all(mixed_part, "seq", split_axis=1, concat_axis=0, tiled=True)
+    mixed = jnp.concatenate(
+        lax.all_to_all(jnp.stack(jnp.split(mixed_part, lax.axis_size("seq"), axis=1)), "seq", 0, 0),
+        axis=0,
+    )
     mixed_form = "cd,ct->dt"
     weight_cols = out_weight
     summed = lax.psum_scatter(

time: 312 us -> 316 us (1.013)
  local copies, waits for them, and re-layouts: 51 us -> 56.2 us
    unnamed x81 -> x88, local copies, waits for them, and re-layouts: 11.6 us -> 16.1 us
  transfers between devices with their start and end apart: 5 -> 5, of which waited for: 3 -> 3; matrix products, arithmetic and copies ran while one was open for 34% -> 33% of each run, Pallas kernels for 0% -> 0%
where the time goes in v1:
time: 316 us
  other arithmetic  104 us (33%)
  local copies, waits for them, and re-layouts  56.2 us (18%)
  waiting for transfers between devices  53.9 us (17%)
  blocking collectives  40.3 us (13%)
  matrix products  34 us (11%)
  between operations  14.6 us (5%)
  starting transfers between devices  12.4 us (4%)
    add x1, other arithmetic, later_taps(): result + weights[delay] * take_rows(extended, delay, out_rows, time_axis)  43.8 us
    mul x1, other arithmetic, body(): query_grad = grad_part * conv  41.9 us
    all_to_all x1, blocking collectives, body(): lax.all_to_all(input_part, 'seq', split_axis=2, concat_axis=1, tiled=True)  40.3 us
    all_to_all x1, waiting for transfers between devices, body(): lax.all_to_all(moved, 'seq', split_axis=1, concat_axis=2, tiled=True)  36 us
    dot_general x1, matrix products, body(): jnp.einsum(grad_form, lax.all_gather(cotangent, 'tp', axis=1, tiled=True)...  18 us
    unnamed x88, local copies, waits for them, and re-layouts  16.1 us
    dot_general x1, matrix products, body(): jnp.einsum(mixed_form, weight_cols, mixed, preferred_element_type=jnp.flo...  16 us
    convert_element_type x1, local copies, waits for them, and re-layouts, backward_core(): later_taps(stacked, feat_weights, row_count, stack_axis)  12 us
  transfers between devices with their start and end apart: 5, of which 3 were waited for; matrix products, arithmetic and copies ran while one was open for 33% of the time, Pallas kernels for 0%

profile of v1, /device:TPU:0, one launch (start us, length us, event | category | flops | bytes accessed | tf_op | source)
XLA Modules:
  0.0 315.6 jit_solution(714221801025335574)
XLA Ops:
  7.9 6.9 %copy.13 = bf16[192,3,2048]{0,1,2:T(4,128)(2,1)} copy(bf16[192,3,2048]{2,0,1:T(8,128)(2,1)} %param.5) | data formatting | bytes 4718592 | tf_op args[0]
  14.9 5.2 %all-to-all-start = ((bf16[3,2048,192]{2,0,1:T(4,128)(2,1)}), bf16[3,2048,192]{2,0,1:T(4,128)(2,1)}, u32[]{:S(2)}, u32[]{:S(2)}) async-start(bf16[3,2048,192]{2,0,1:T(4,128)(2,1)} %bitcast.99), calls=%async_computation | async-start | bytes 8388608 | tf_op jit(solution)/shard_map/all_to_all | solution.py:70
  25.3 2.0 slice_reduce_fusion.126
  27.3 2.0 slice_reduce_fusion.125
  29.3 2.0 slice_reduce_fusion.124
  31.3 2.0 slice_reduce_fusion.123
  33.3 36.0 %all-to-all-done = bf16[3,2048,192]{2,0,1:T(4,128)(2,1)} async-done(((bf16[3,2048,192]{2,0,1:T(4,128)(2,1)}), bf16[3,2048,192]{2,0,1:T(4,128)(2,1)}, u32[]{:S(2)}, u32[]{:S(2)}) %all-to-all-start) | async-done | bytes 2359328 | tf_op jit(solution)/shard_map/all_to_all | solution.py:70
  69.3 6.9 %copy.22 = bf16[3,8,256,192]{2,3,1,0:T(8,128)(2,1)} copy(bf16[3,8,256,192]{3,0,2,1:T(4,128)(2,1)} %bitcast.1) | data formatting | bytes 4718592 | tf_op jit(solution)/shard_map/all_to_all | solution.py:70
  76.2 18.0 %fusion.151 = f32[2048,192]{0,1:T(8,128)S(1)} fusion(bf16[2048,8192]{1,0:T(8,128)(2,1)} %param.8, bf16[192,8192]{1,0:T(8,128)(2,1)} %all-gather.2.cloned.1.call-done), kind=kOutput, calls=%fused_computation.454 | convolution fusion | flops 6442450944 | bytes 38273024 | tf_op jit(solution)/shard_map/te,ce->ct/dot_general | solution.py:96
  95.5 3.6 %all-to-all-start.2 = ((f32[8,256,192]{1,2,0:T(8,128)}), f32[8,256,192]{1,2,0:T(8,128)S(1)}, u32[]{:S(2)}, u32[]{:S(2)}) async-start(f32[8,256,192]{1,2,0:T(8,128)} %bitcast.97), calls=%async_computation.3 | async-start | bytes 3145728 | tf_op jit(solution)/shard_map/all_to_all | solution.py:102
  99.1 10.0 %multiply_add_fusion = f32[3,256,1663]{1,2,0:T(8,128)S(1)} fusion(f32[3,256]{1,0:T(4,128)S(1)} %get-tuple-element.145, f32[3,256]{1,0:T(4,128)S(1)} %get-tuple-element.146, f32[3,256]{1,0:T(4,128)S(1)} %get-tuple-element.147, f32[3,256]{1,0:T(4,128)S(1)} %get-tuple-element.148, f32[3,256]{1,0:T(4,128)S(1)} %get-tuple-element.149, ...), kind=kLoop, calls=%fused_computation.2 | loop fusion | flops 25543680 | bytes 7489536 | tf_op jit(solution)/shard_map/add | solution.py:19
  109.1 2.2 copy-done.2
  111.6 8.4 %all-to-all-done.2 = f32[8,256,192]{1,2,0:T(8,128)S(1)} async-done(((f32[8,256,192]{1,2,0:T(8,128)}), f32[8,256,192]{1,2,0:T(8,128)S(1)}, u32[]{:S(2)}, u32[]{:S(2)}) %all-to-all-start.2) | async-done | bytes 1572896 | tf_op jit(solution)/shard_map/all_to_all | solution.py:102
  120.0 41.9 %bitcast_multiply_fusion.1 = (f32[256,1536]{0,1:T(8,128)}, f32[256,1536]{0,1:T(8,128)}) fusion(f32[8,256,192]{1,2,0:T(8,128)S(1)} %all-to-all-done.2, f32[256,1663]{0,1:T(8,128)S(1)} %fusion.8, f32[256]{0:T(256)S(1)} %get-tuple-element.3, f32[256]{0:T(256)S(1)} %get-tuple-element.4, f32[256]{0:T(256)S(1)} %get-tuple-element.5, f32[256]{0:T(256)S(1)} %get-tuple-element.6, ...), kind=kLoop, calls=%fused_computation.283 | loop fusion | flops 100663296 | bytes 206176256 | tf_op jit(solution)/shard_map/mul | solution.py:104
  161.9 2.3 bitcast_multiply_fusion
  169.5 3.5 %all-to-all-start.1 = ((bf16[8,256,192]{1,2,0:T(8,128)(2,1)}), bf16[8,256,192]{1,2,0:T(8,128)(2,1)S(1)}, u32[]{:S(2)}, u32[]{:S(2)}) async-start(bf16[8,256,192]{1,2,0:T(8,128)(2,1)} %fusion.142), calls=%async_computation.1 | async-start | bytes 1572864 | tf_op jit(solution)/shard_map/all_to_all | solution.py:80
  173.1 3.7 %slice_bitcast_fusion.1 = (f32[256,1536]{0,1:T(8,128)}, f32[256,1536]{0,1:T(8,128)}) fusion(f32[3,256,1663]{1,2,0:T(8,128)} %copy-done.2), kind=kLoop, calls=%fused_computation.25 | loop fusion | bytes 6291456 | tf_op jit(solution)/shard_map/squeeze | solution.py:12
  176.8 8.7 %all-to-all-done.1 = bf16[8,256,192]{1,2,0:T(8,128)(2,1)S(1)} async-done(((bf16[8,256,192]{1,2,0:T(8,128)(2,1)}), bf16[8,256,192]{1,2,0:T(8,128)(2,1)S(1)}, u32[]{:S(2)}, u32[]{:S(2)}) %all-to-all-start.1) | async-done | bytes 786464 | tf_op jit(solution)/shard_map/all_to_all | solution.py:80
  185.6 16.0 %fusion = bf16[8192,192]{0,1:T(8,128)(2,1)} fusion(bf16[2048,192]{0,1:T(8,128)(2,1)S(1)} %bitcast.106, bf16[2048,8192]{1,0:T(8,128)(2,1)} %param.8), kind=kOutput, calls=%fused_computation.1 | convolution fusion | flops 6444023808 | bytes 37486592 | tf_op jit(solution)/shard_map/cd,ct->dt/dot_general | solution.py:86
  202.5 43.8 %multiply_add_fusion.1 = f32[256,1536]{0,1:T(8,128)} fusion(f32[256,1536]{0,1:T(8,128)S(1)} %get-tuple-element.134, f32[256]{0:T(256)S(1)} %get-tuple-element.3, f32[256]{0:T(256)S(1)} %get-tuple-element.4, f32[256]{0:T(256)S(1)} %get-tuple-element.5, f32[256]{0:T(256)S(1)} %get-tuple-element.6, f32[256]{0:T(256)S(1)} %get-tuple-element.7, ...), kind=kLoop, calls=%fused_computation.284 | loop fusion | flops 100270080 | bytes 3276800 | tf_op jit(solution)/shard_map/add | solution.py:28
  250.3 4.0 %fusion.2 = bf16[3,256,1536]{1,2,0:T(8,128)(2,1)S(1)} fusion(f32[3,256,1542]{1,2,0:T(8,128)S(1)} %pad_maximum_fusion, f32[3,256]{1,0:T(4,128)S(1)} %get-tuple-element.145, f32[3,256]{1,0:T(4,128)S(1)} %get-tuple-element.146, f32[3,256]{1,0:T(4,128)S(1)} %get-tuple-element.147, f32[3,256]{1,0:T(4,128)S(1)} %get-tuple-element.148, ...), kind=kLoop, calls=%fused_computation.6 | loop fusion | flops 16515072 | bytes 35410944 | tf_op jit(solution)/shard_map/convert_element_type | solution.py:56
  254.3 12.0 %copy.18 = bf16[3,256,1536]{1,0,2:T(4,128)(2,1)S(1)} copy(bf16[3,256,1536]{1,2,0:T(8,128)(2,1)S(1)} %fusion.2) | data formatting | bytes 4718592 | tf_op jit(solution)/shard_map/convert_element_type | solution.py:56
  266.4 40.3 %all_to_all.60 = bf16[3,256,1536]{1,0,2:T(4,128)(2,1)S(1)} all-to-all(bf16[3,256,1536]{1,0,2:T(4,128)(2,1)S(1)} %copy.18), channel_id=1, replica_groups=mesh['seq'=8,'tp'=4] {'seq'}, dimensions={2} | all-to-all | bytes 4718592 | tf_op jit(solution)/shard_map/all_to_all | solution.py:117
  307.0 1.7 copy.32
  (106 shorter events, 17.7 us)
Async XLA Ops:
  7.2 14.1 %copy-start = (f32[128,128]{1,0:T(8,128)S(1)}, f32[128,128]{1,0:T(8,128)}, u32[]{:S(2)}) copy-start(f32[128,128]{1,0:T(8,128)} %param.7) | copy-start | bytes 196612
  7.2 69.0 %all-gather.2.cloned.1.call-start = ((), (), s32[]{:S(2)}) async-start(), calls=%async_computation.6 | async-start | bytes 3932160 | tf_op jit(solution)/shard_map/all_gather | solution.py:98
  14.9 54.4 %all-to-all-start = ((bf16[3,2048,192]{2,0,1:T(4,128)(2,1)}), bf16[3,2048,192]{2,0,1:T(4,128)(2,1)}, u32[]{:S(2)}, u32[]{:S(2)}) async-start(bf16[3,2048,192]{2,0,1:T(4,128)(2,1)} %bitcast.99), calls=%async_computation | async-start | bytes 8388608 | tf_op jit(solution)/shard_map/all_to_all | solution.py:70
  95.5 24.5 %all-to-all-start.2 = ((f32[8,256,192]{1,2,0:T(8,128)}), f32[8,256,192]{1,2,0:T(8,128)S(1)}, u32[]{:S(2)}, u32[]{:S(2)}) async-start(f32[8,256,192]{1,2,0:T(8,128)} %bitcast.97), calls=%async_computation.3 | async-start | bytes 3145728 | tf_op jit(solution)/shard_map/all_to_all | solution.py:102
  109.1 2.3 copy-start.2
  169.5 16.1 %all-to-all-start.1 = ((bf16[8,256,192]{1,2,0:T(8,128)(2,1)}), bf16[8,256,192]{1,2,0:T(8,128)(2,1)S(1)}, u32[]{:S(2)}, u32[]{:S(2)}) async-start(bf16[8,256,192]{1,2,0:T(8,128)(2,1)} %fusion.142), calls=%async_computation.1 | async-start | bytes 1572864 | tf_op jit(solution)/shard_map/all_to_all | solution.py:80
  173.0 135.7 %reduce-scatter.2.cloned.1.call-start = ((), (), s32[]{:S(2)}) async-start(), calls=%async_computation.5 | async-start | bytes 3932160 | tf_op jit(solution)/shard_map/reduce_scatter | solution.py:85
  201.6 0.7 copy-start.9
  201.6 0.7 copy-start.10
  201.6 0.7 copy-start.11
  201.6 0.7 copy-start.12
  201.6 0.7 copy-start.13
  201.6 0.7 copy-start.14
  201.6 0.7 copy-start.15
  201.6 0.7 copy-start.16
  201.7 0.7 copy-start.19
  201.8 0.7 copy-start.33
  201.8 0.7 copy-start.34
  201.8 0.7 copy-start.35
  201.9 0.7 copy-start.37
  202.5 43.8 %copy-start.3 = (f32[256,1536]{0,1:T(8,128)S(1)}, f32[256,1536]{0,1:T(8,128)}, u32[]{:S(2)}) copy-start(f32[256,1536]{0,1:T(8,128)} %get-tuple-element.130) | copy-start | bytes 4718596
  246.3 1.4 copy-start.4
  246.3 1.9 copy-start.5
  307.0 1.7 copy-start.1
  (19 other events, 12.6 us)
Sparse Core Ops, SparseCore 0:
  9.6 66.1 all-gather.1
  202.0 60.5 reduce-scatter.1
